TPU v7x, 256 devices: a whole 4x4x8 slice. The times are simulated.
256 devices in a mesh: section: 4 (over z_lo, core), seq: 64 (over y, x, z_hi).
Axes of the slice: x: 4, y: 4, z: 8 (z_hi: 4, z_lo: 2; z = z_hi * 2 + z_lo), core: 2. Of those that a mesh axis runs over, the one named last changes fastest.
Arguments:
- q_img: bfloat16 [8192, 3072], P('seq', 'section'), may hold values from -6 to 6
- k_img: bfloat16 [8192, 3072], P('seq', 'section'), may hold values from -6 to 6
- v_img: bfloat16 [8192, 3072], P('seq', 'section'), may hold values from -6 to 6
- q_txt: bfloat16 [256, 3072], P('seq', 'section'), may hold values from -6 to 6
- k_txt: bfloat16 [256, 3072], P('seq', 'section'), may hold values from -6 to 6
- v_txt: bfloat16 [256, 3072], P('seq', 'section'), may hold values from -6 to 6
- norm_gains: float32 [4, 128], replicated, may hold values from 1.2 to 2
- block_map: int32 [24, 64, 64], P('section', 'seq'), may hold values 0 or 1
Outputs:
- image_out: bfloat16 [2048, 4, 3072], P('seq', 'section')
- text_out: bfloat16 [256, 3072], P('seq', 'section')
All inputs are finite; a program needn't handle non-finite values. No bound on the sum of `block_map` on one device may be relied on, other than what follows from the above.
Results may differ from a plain program's by a relative error of at most 0.011.
Values may be sent and summed in bfloat16 or wider, within the bound.
No kernel may reach another device: no remote copies, remote signals or barrier semaphores. Data moves between devices by JAX's collectives and lax.ppermute only.
A program may use at most 256 MiB of HBM per device.

v0:
```python
import jax
import jax.numpy as jnp
from jax import lax
from jax.sharding import PartitionSpec as P

BLOCK = 128


def normed(values, gain, heads):
    rows = values.shape[0]
    floats = values.astype(jnp.float32).reshape(rows, heads, gain.shape[0])
    power = jnp.mean(floats * floats, axis=-1, keepdims=True)
    return (floats * lax.rsqrt(power + 1e-06) * gain).astype(jnp.bfloat16)


def make_keep(flags, query_shards, shards, first, rows, text_rows):
    heads = flags.shape[0]
    key_blocks = rows // BLOCK
    stride = rows + text_rows
    picked = lax.dynamic_slice_in_dim(flags, first * key_blocks, shards * key_blocks, 2)
    picked = picked.reshape(heads, query_shards, key_blocks, shards, key_blocks)
    image_mask = jnp.broadcast_to(
        picked[:, :, :, None, :, :, None] > 0,
        (heads, query_shards, key_blocks, BLOCK, shards, key_blocks, BLOCK),
    )
    image_mask = image_mask.reshape(heads, query_shards, rows, shards, rows)
    keep = jnp.pad(
        image_mask, ((0, 0), (0, 0), (0, text_rows), (0, 0), (0, text_rows)), constant_values=True
    )
    return keep.reshape(heads, query_shards * stride, shards, stride)


def accumulate(queries, flags, query_shards, rows, text_rows, carry, pieces, start):
    numer, denom = carry
    piece_keys, piece_values = pieces
    heads = queries.shape[1]
    head_size = queries.shape[2]
    stride = rows + text_rows
    shards = piece_keys.shape[0] // stride
    first = start // stride
    keys_four = piece_keys.reshape(shards, stride, heads, head_size)
    values_four = piece_values.reshape(shards, stride, heads, head_size)
    scores = jnp.einsum(
        "qhd,skhd->hqsk", queries, keys_four, preferred_element_type=jnp.float32
    ) * head_size ** (-0.5)
    keep = make_keep(flags, query_shards, shards, first, rows, text_rows)
    weights = jnp.where(keep, jnp.exp(scores), jnp.float32(0.0))
    denom = denom + jnp.sum(weights, axis=(2, 3))
    numer = numer + jnp.einsum(
        "hqsk,skhd->hqd",
        weights.astype(jnp.bfloat16),
        values_four,
        preferred_element_type=jnp.float32,
    )
    return (numer, denom)


def body(q_img, k_img, v_img, q_txt, k_txt, v_txt, norm_gains, block_map):
    rows, width = q_img.shape
    head_size = norm_gains.shape[1]
    heads = width // head_size
    text_rows = q_txt.shape[0]
    stride = rows + text_rows
    queries = jnp.concatenate(
        [normed(q_img, norm_gains[0], heads), normed(q_txt, norm_gains[2], heads)], axis=0
    )
    keys_image = normed(k_img, norm_gains[1], heads).reshape(rows, width)
    keys_text = normed(k_txt, norm_gains[3], heads).reshape(text_rows, width)
    local_keys = jnp.concatenate([keys_image, keys_text], axis=0)
    local_values = jnp.concatenate([v_img, v_txt], axis=0)
    start_state = (
        jnp.zeros((heads, stride, head_size), jnp.float32),
        jnp.zeros((heads, stride), jnp.float32),
    )

    def fold_step(carry, pieces, start):
        return accumulate(queries, block_map, 1, rows, text_rows, carry, pieces, start)

    whole_keys, whole_values = (
        lax.all_gather(local_keys, "seq", axis=0, tiled=True),
        lax.all_gather(local_values, "seq", axis=0, tiled=True),
    )
    count_seq = lax.axis_size("seq")
    grouped = 1
    while (
        grouped * 2 <= count_seq
        and count_seq % (grouped * 2) == 0
        and (grouped * 2 * stride <= 1024)
    ):
        grouped = grouped * 2
    span = grouped * stride

    def step_over(index, carry):
        offset = index * span
        piece_keys = lax.dynamic_slice_in_dim(whole_keys, offset, span, 0)
        piece_values = lax.dynamic_slice_in_dim(whole_values, offset, span, 0)
        return fold_step(carry, (piece_keys, piece_values), offset)

    numer, denom = lax.fori_loop(0, count_seq // grouped, step_over, start_state)
    result = numer / denom[..., None]
    merged = result.transpose(1, 0, 2).reshape(stride, width).astype(jnp.bfloat16)
    image_part = merged[:rows]
    text_out = merged[rows:]
    sections = lax.axis_size("section")
    image_out = lax.all_to_all(
        image_part.reshape(rows // sections, sections, width),
        "section",
        split_axis=1,
        concat_axis=2,
        tiled=True,
    )
    return (image_out, text_out)


def solution(mesh):
    placed = (
        P("seq", "section"),
        P("seq", "section"),
        P("seq", "section"),
        P("seq", "section"),
        P("seq", "section"),
        P("seq", "section"),
        P(),
        P("section", "seq", None),
    )
    return jax.shard_map(
        body,
        mesh=mesh,
        in_specs=placed,
        out_specs=(P("seq", "section", None), P("seq", "section")),
        check_vma=False,
    )
```

profile of v0, /device:TPU:4, one launch (start us, length us, event | category | flops | bytes accessed | tf_op | source)
XLA Modules:
  0.0 707.3 jit_solution(929896019080219932)
XLA Ops:
  14.1 136.7 %all-gather.5.cloned.1.call-done = bf16[64,132,768]{2,1,0:T(8,128)(2,1)} async-done(((bf16[1,132,768]{2,1,0:T(8,128)(2,1)}), bf16[64,132,768]{2,1,0:T(8,128)(2,1)}) %all-gather.5.cloned.1.call-update) | async-done | bytes 12976144 | tf_op jit(solution)/shard_map/all_gather | solution.py:80
  150.8 16.0 %reshape.141 = bf16[8448,768]{1,0:T(8,128)(2,1)} reshape(bf16[64,132,768]{2,1,0:T(8,128)(2,1)} %all-gather.5.cloned.1.call-done) | data formatting | bytes 25952256
  166.8 131.9 %all-gather.7.cloned.1.call-done = bf16[64,132,768]{2,1,0:T(8,128)(2,1)} async-done(((bf16[1,132,768]{2,1,0:T(8,128)(2,1)}), bf16[64,132,768]{2,1,0:T(8,128)(2,1)}) %all-gather.7.cloned.1.call-update) | async-done | bytes 12976144 | tf_op jit(solution)/shard_map/all_gather | solution.py:81
  298.7 16.1 %reshape.143 = bf16[8448,768]{1,0:T(8,128)(2,1)} reshape(bf16[64,132,768]{2,1,0:T(8,128)(2,1)} %all-gather.7.cloned.1.call-done) | data formatting | bytes 25952256
  314.8 363.8 %while.18 = (s32[]{:T(128)}, f32[6,132,128]{2,1,0:T(8,128)}, f32[6,132]{1,0:T(8,128)S(1)}, s32[6,1,64]{0,2,1:T(8,128)S(1)}, bf16[8448,768]{1,0:T(8,128)(2,1)}, /...) while((s32[]{:T(128)}, f32[6,132,128]{2,1,0:T(8,128)}, ...), condition=%wide.region_6.7_spmd.clone, body=%wide.region_4.6_spmd.clone.sunk | while | flops 215982384 | bytes 21925776 | solution.py:99
  321.6 4.7 copy.123
  344.2 4.7 copy.123
  354.9 3.3 fusion.36
  367.0 4.7 copy.123
  389.7 4.7 copy.123
  412.5 4.7 copy.123
  435.2 4.7 copy.123
  458.0 4.7 copy.123
  480.7 4.7 copy.123
  503.5 4.7 copy.123
  526.2 4.7 copy.123
  549.0 4.7 copy.123
  571.7 4.7 copy.123
  594.4 4.7 copy.123
  617.2 4.7 copy.123
  639.9 4.7 copy.123
  662.7 4.7 copy.123
  680.8 13.4 %all-to-all-start = ((bf16[32,4,768]{2,0,1:T(8,128)(2,1)}), bf16[32,4,768]{2,0,1:T(8,128)(2,1)S(1)}, u32[]{:S(2)}, u32[]{:S(2)}) async-start(bf16[32,4,768]{2,0,1:T(8,128)(2,1)} %copy.97), calls=%async_computation | async-start | bytes 393216 | tf_op jit(solution)/shard_map/all_to_all | solution.py:105
  694.7 4.7 all-to-all-done
  (259 shorter events, 294.4 us)
Async XLA Ops:
  7.2 5.1 copy-start.1
  7.2 5.1 copy-start.3
  7.2 5.8 copy-start.4
  7.2 6.0 copy-start.2
  7.2 143.6 %all-gather.5.cloned.1.call-start = ((), (), s32[]{:S(2)}) async-start(), calls=%async_computation.1 | async-start | bytes 13578240 | tf_op jit(solution)/shard_map/all_gather | solution.py:80
  11.1 2.9 copy-start.5
  12.2 286.5 %all-gather.7.cloned.1.call-start = ((), (), s32[]{:S(2)}) async-start(), calls=%async_computation.2 | async-start | bytes 13578240 | tf_op jit(solution)/shard_map/all_gather | solution.py:81
  332.2 3.2 copy-start
  354.9 3.3 copy-start
  377.6 3.3 copy-start
  400.4 3.3 copy-start
  423.1 3.3 copy-start
  445.9 3.3 copy-start
  468.6 3.3 copy-start
  491.4 3.3 copy-start
  514.1 3.3 copy-start
  536.9 3.3 copy-start
  559.6 3.3 copy-start
  582.3 3.3 copy-start
  605.1 3.3 copy-start
  627.8 3.3 copy-start
  650.6 3.3 copy-start
  673.3 3.3 copy-start
  680.8 18.7 %all-to-all-start = ((bf16[32,4,768]{2,0,1:T(8,128)(2,1)}), bf16[32,4,768]{2,0,1:T(8,128)(2,1)S(1)}, u32[]{:S(2)}, u32[]{:S(2)}) async-start(bf16[32,4,768]{2,0,1:T(8,128)(2,1)} %copy.97), calls=%async_computation | async-start | bytes 393216 | tf_op jit(solution)/shard_map/all_to_all | solution.py:105
Sparse Core Ops, SparseCore 0:
  12.3 138.4 all-gather.4
  154.1 144.5 all-gather.6
where the time goes:
time: 711 us; the launch traced here: 707 us
  waiting for transfers between devices  273 us (38%)
  local copies, waits for them, and re-layouts  229 us (32%)
  matrix products  89.9 us (13%)
  other arithmetic  86 us (12%)
  between operations  14.3 us (2%)
  starting transfers between devices  13.5 us (2%)
    all_gather x1, waiting for transfers between devices, body(): lax.all_gather(local_keys, 'seq', axis=0, tiled=True)  137 us
    all_gather x1, waiting for transfers between devices, body(): lax.all_gather(local_values, 'seq', axis=0, tiled=True)  132 us
    while x48, local copies, waits for them, and re-layouts  75.5 us
    dot_general x16, matrix products, accumulate(): jnp.einsum('hqsk,skhd->hqd', weights.astype(jnp.bfloat16), values_four, p...  52.2 us
    convert_element_type x16, other arithmetic, accumulate(): weights.astype(jnp.bfloat16)  50.4 us
    reshape x16, local copies, waits for them, and re-layouts, accumulate(): values_four = piece_values.reshape(shards, stride, heads, head_size)  44.4 us
    dynamic_slice x16, local copies, waits for them, and re-layouts, step_over(): piece_values = lax.dynamic_slice_in_dim(whole_values, offset, span, 0)  38.4 us
    dot_general x16, matrix products, accumulate(): jnp.einsum('qhd,skhd->hqsk', queries, keys_four, preferred_element_type=j...  37.6 us
  transfers between devices with their start and end apart: 3, of which 3 were waited for; matrix products, arithmetic and copies ran while one was open for 3% of the time, Pallas kernels for 0%

commit v1 on v0

--- a/solution.py
+++ b/solution.py
@@ -76,9 +76,18 @@
     def fold_step(carry, pieces, start):
         return accumulate(queries, block_map, 1, rows, text_rows, carry, pieces, start)
 
+    def guide_orders_here(state, link_axis):
+        raw_out = lax.all_to_all(
+            jnp.stack([state for _ in range(lax.axis_size(link_axis))], 0),
+            link_axis,
+            concat_axis=0,
+            split_axis=0,
+        )
+        return jnp.concatenate(raw_out, 0)
+
     whole_keys, whole_values = (
         lax.all_gather(local_keys, "seq", axis=0, tiled=True),
-        lax.all_gather(local_values, "seq", axis=0, tiled=True),
+        guide_orders_here(local_values, "seq"),
     )
     count_seq = lax.axis_size("seq")
     grouped = 1

time: 711 us -> 843 us (1.19); the launches traced: 707 us -> 829 us
  waiting for transfers between devices: 273 us -> 385 us
    all_gather x1, waiting for transfers between devices: 137 us -> 380 us  [body(): lax.all_gather(local_keys, 'seq', axis=0, tiled=True)]
    all_gather x1 -> x0, waiting for transfers between devices: 132 us -> none  [body(): lax.all_gather(local_values, 'seq', axis=0, tiled=True)]
    reshape x0 -> x1, local copies, waits for them, and re-layouts: none -> 16.1 us  [guide_orders_here(): return jnp.concatenate(raw_out, 0)]
    unnamed x18 -> x17, local copies, waits for them, and re-layouts: 34.6 us -> 18.5 us
    all_to_all x0 -> x1, starting transfers between devices: none -> 14.9 us  [guide_orders_here(): lax.all_to_all(jnp.stack([state for _ in range(lax.axis_size(link_axis))]...]
    all_to_all x1, starting transfers between devices: 13.4 us -> 4.53 us  [body(): lax.all_to_all(image_part.reshape(rows // sections, sections, width), 'se...]
  transfers between devices with their start and end apart: 3 -> 3, of which waited for: 3 -> 2; matrix products, arithmetic and copies ran while one was open for 3% -> 3% of each run, Pallas kernels for 0% -> 0%
where the time goes in v1:
time: 843 us; the launch traced here: 829 us
  waiting for transfers between devices  385 us (46%)
  local copies, waits for them, and re-layouts  235 us (28%)
  matrix products  89.3 us (11%)
  other arithmetic  85.4 us (10%)
  starting transfers between devices  19.5 us (2%)
  between operations  14.3 us (2%)
    all_gather x1, waiting for transfers between devices, body(): lax.all_gather(local_keys, 'seq', axis=0, tiled=True)  380 us
    while x48, local copies, waits for them, and re-layouts  75.5 us
    dot_general x16, matrix products, accumulate(): jnp.einsum('hqsk,skhd->hqd', weights.astype(jnp.bfloat16), values_four, p...  51.9 us
    convert_element_type x16, other arithmetic, accumulate(): weights.astype(jnp.bfloat16)  50.4 us
    reshape x16, local copies, waits for them, and re-layouts, accumulate(): values_four = piece_values.reshape(shards, stride, heads, head_size)  44.4 us
    dynamic_slice x16, local copies, waits for them, and re-layouts, step_over(): piece_values = lax.dynamic_slice_in_dim(whole_values, offset, span, 0)  38.5 us
    dot_general x16, matrix products, accumulate(): jnp.einsum('qhd,skhd->hqsk', queries, keys_four, preferred_element_type=j...  37.4 us
    reduce_sum x16, other arithmetic, accumulate(): denom = denom + jnp.sum(weights, axis=(2, 3))  31.2 us
  transfers between devices with their start and end apart: 3, of which 2 were waited for; matrix products, arithmetic and copies ran while one was open for 3% of the time, Pallas kernels for 0%

profile of v1, /device:TPU:4, one launch (start us, length us, event | category | flops | bytes accessed | tf_op | source)
XLA Modules:
  0.0 829.3 jit_solution(11356613401572251958)
XLA Ops:
  12.2 5.6 stack.2
  17.8 14.9 %all-to-all-start = ((bf16[64,132,768]{2,1,0:T(8,128)(2,1)}), bf16[64,132,768]{2,1,0:T(8,128)(2,1)}, u32[]{:S(2)}, u32[]{:S(2)}) async-start(bf16[64,132,768]{2,1,0:T(8,128)(2,1)} %stack.2), calls=%async_computation | async-start | bytes 26738688 | tf_op jit(solution)/shard_map/all_to_all | solution.py:80
  33.9 380.0 %all-gather.3.cloned.1.call-done = bf16[64,132,768]{2,1,0:T(8,128)(2,1)} async-done(((bf16[1,132,768]{2,1,0:T(8,128)(2,1)}), bf16[64,132,768]{2,1,0:T(8,128)(2,1)}) %all-gather.3.cloned.1.call-update) | async-done | bytes 12976144 | tf_op jit(solution)/shard_map/all_gather | solution.py:89
  413.9 16.1 %reshape.147 = bf16[8448,768]{1,0:T(8,128)(2,1)} reshape(bf16[64,132,768]{2,1,0:T(8,128)(2,1)} %all-gather.3.cloned.1.call-done) | data formatting | bytes 25952256
  429.9 16.1 %reshape.140 = bf16[8448,768]{1,0:T(8,128)(2,1)} reshape(bf16[64,132,768]{2,1,0:T(8,128)(2,1)} %all-to-all-done) | data formatting | bytes 25952256 | tf_op jit(solution)/shard_map/reshape | solution.py:86
  446.1 363.4 %while.18 = (s32[]{:T(128)}, f32[6,132,128]{2,1,0:T(8,128)}, f32[6,132]{1,0:T(8,128)S(1)}, s32[6,1,64]{0,2,1:T(8,128)S(1)}, bf16[8448,768]{1,0:T(8,128)(2,1)}, /...) while((s32[]{:T(128)}, f32[6,132,128]{2,1,0:T(8,128)}, ...), condition=%wide.region_6.7_spmd.clone, body=%wide.region_4.6_spmd.clone.sunk | while | flops 215982384 | bytes 21925776 | solution.py:108
  452.9 4.7 copy.123
  475.5 4.7 copy.123
  498.2 4.7 copy.123
  520.9 4.7 copy.123
  543.7 4.7 copy.123
  566.4 4.7 copy.123
  589.1 4.7 copy.123
  611.8 4.7 copy.123
  634.5 4.7 copy.123
  657.3 4.7 copy.123
  680.0 4.7 copy.123
  702.7 4.7 copy.123
  725.4 4.7 copy.123
  748.1 4.7 copy.123
  770.9 4.7 copy.123
  793.6 4.7 copy.123
  811.6 4.5 all-to-all-start.1
  816.8 4.7 all-to-all-done.1
  (259 shorter events, 296.5 us)
Async XLA Ops:
  7.2 5.0 copy-start.1
  7.2 5.0 copy-start.3
  7.2 406.7 %all-gather.3.cloned.1.call-start = ((), (), s32[]{:S(2)}) async-start(), calls=%async_computation.2 | async-start | bytes 13578240 | tf_op jit(solution)/shard_map/all_gather | solution.py:89
  17.8 15.0 %copy-start.4 = (bf16[4,768]{1,0:T(4,128)(2,1)S(1)}, bf16[4,768]{1,0:T(4,128)(2,1)}, u32[]{:S(2)}) copy-start(bf16[4,768]{1,0:T(4,128)(2,1)} %param.13) | copy-start | bytes 18436
  17.8 15.1 %copy-start.2 = (bf16[128,768]{1,0:T(8,128)(2,1)S(1)}, bf16[128,768]{1,0:T(8,128)(2,1)}, u32[]{:S(2)}) copy-start(bf16[128,768]{1,0:T(8,128)(2,1)} %param.10) | copy-start | bytes 589828
  17.8 412.1 %all-to-all-start = ((bf16[64,132,768]{2,1,0:T(8,128)(2,1)}), bf16[64,132,768]{2,1,0:T(8,128)(2,1)}, u32[]{:S(2)}, u32[]{:S(2)}) async-start(bf16[64,132,768]{2,1,0:T(8,128)(2,1)} %stack.2), calls=%async_computation | async-start | bytes 26738688 | tf_op jit(solution)/shard_map/all_to_all | solution.py:80
  32.7 1.0 copy-start.5
  463.5 3.2 copy-start
  486.1 3.3 copy-start
  508.9 3.3 copy-start
  531.6 3.3 copy-start
  554.3 3.3 copy-start
  577.0 3.3 copy-start
  599.7 3.3 copy-start
  622.5 3.3 copy-start
  645.2 3.3 copy-start
  667.9 3.3 copy-start
  690.6 3.3 copy-start
  713.3 3.3 copy-start
  736.1 3.3 copy-start
  758.8 3.3 copy-start
  781.5 3.3 copy-start
  804.2 3.3 copy-start
  811.6 9.8 %all-to-all-start.1 = ((bf16[32,4,768]{2,0,1:T(8,128)(2,1)}), bf16[32,4,768]{2,0,1:T(8,128)(2,1)S(1)}, u32[]{:S(2)}, u32[]{:S(2)}) async-start(bf16[32,4,768]{2,0,1:T(8,128)(2,1)} %copy.97), calls=%async_computation.1 | async-start | bytes 393216 | tf_op jit(solution)/shard_map/all_to_all | solution.py:114
Sparse Core Ops, SparseCore 0:
  12.3 401.5 all-gather.2
